TPU v7x, 512 devices: a whole 4x4x16 slice. The times are simulated.
512 devices in a mesh: expert: 8 (over y, core), mp: 64 (over x, z).
Axes of the slice: x: 4, y: 4, z: 16, core: 2. Of those that a mesh axis runs over, the one named last changes fastest.
Arguments:
- context: bfloat16 [4096, 2048], P('expert', 'mp'), may hold values from -6 to 6
- out_proj: bfloat16 [2048, 2048], P('mp'), may hold values from -1 to 1, as said below
- routes: int32 [4096, 2], P('expert'), may hold values from 0 to 7, all different within a row; in each aligned block of 512 rows (0 to 511, 512 to 1023, ...) at most 256 rows name the same one
- router_logits: float32 [4096, 2], P('expert'), may hold values from -8 to 8
- w_gate: bfloat16 [45056, 2048], P('mp', 'expert'), may hold values from -0.125 to 0.125
- w_up: bfloat16 [45056, 2048], P('mp', 'expert'), may hold values from -0.125 to 0.125
- w_down: bfloat16 [45056, 2048], P('mp', 'expert'), may hold values from -0.078125 to 0.078125
- norm_gain: float32 [2048], P('mp'), may hold values from 0.25 to 1.75
- request_order: int32 [4096], P('expert'), may hold values from 0 to 4095, each once
Outputs:
- restored: bfloat16 [4096, 2048], P('expert', 'mp')
Inputs may be any that keep to these rules, and one draw needn't show every extreme that they name: `routes`: each row names 2 different experts. Within each aligned block of 512 rows no expert is named by more than 256 rows, and in some blocks one expert is named by exactly 256 rows. `request_order`: A permutation of the 4096 token rows. `out_proj`: entries of the order of one over the square root of 2048.
All inputs are finite; a program needn't handle non-finite values.
Results may differ from a plain program's by a relative error of at most 0.0056.
Values may be sent and summed in bfloat16 or wider, within the bound.
No kernel may reach another device: no remote copies, remote signals or barrier semaphores. Data moves between devices by JAX's collectives and lax.ppermute only.
A program may use at most 64 MiB of HBM per device.

v0:
```python
import jax
import jax.numpy as jnp
from jax import lax
from jax.sharding import PartitionSpec as P

EXPERTS = 8
CAP = 256
epsilon = 1e-06


def slot_targets(routes, capacity, experts):
    flat_routes = routes.reshape(-1)
    onehot = (flat_routes[:, None] == jnp.arange(experts, dtype=jnp.int32)[None, :]).astype(
        jnp.int32
    )
    earlier = jnp.cumsum(onehot, axis=0) - onehot
    slot_index = jnp.sum(earlier * onehot, axis=1)
    return flat_routes * capacity + slot_index


def shards(
    context, out_proj, routes, router_logits, w_gate, w_up, w_down, norm_gain, request_order
):
    tok_rows = context.shape[0]
    feat_local = context.shape[1]
    model_width = out_proj.shape[1]
    mp_count = lax.axis_size("mp")
    copies = mp_count // EXPERTS
    capacity = CAP
    top_k = routes.shape[1]
    attended = jnp.einsum(
        "td,cd->tc",
        lax.all_gather(context, "mp", axis=1, tiled=True),
        out_proj,
        preferred_element_type=jnp.float32,
    ).astype(jnp.bfloat16)
    destination = slot_targets(routes, capacity, EXPERTS)
    source_rows = jnp.repeat(jnp.arange(tok_rows, dtype=jnp.int32), top_k)
    slotted = (
        jnp.zeros((EXPERTS * capacity, feat_local), jnp.bfloat16)
        .at[destination]
        .set(attended[source_rows])
    )
    slotted = jnp.repeat(slotted.reshape(EXPERTS, capacity, feat_local), copies, axis=0)
    outgoing = slotted.transpose(1, 0, 2).reshape(capacity, mp_count * feat_local)
    inbox_rows = lax.all_to_all(outgoing, "mp", split_axis=1, concat_axis=1, tiled=True)
    gate_next = jnp.einsum(
        "rd,hd->rh",
        inbox_rows,
        lax.all_gather(w_gate, "expert", axis=1, tiled=True),
        preferred_element_type=jnp.float32,
    )
    up_next = jnp.einsum(
        "rd,hd->rh",
        inbox_rows,
        lax.all_gather(w_up, "expert", axis=1, tiled=True),
        preferred_element_type=jnp.float32,
    )
    activated = (jax.nn.silu(gate_next) * up_next).astype(jnp.bfloat16)
    partial_value = jnp.dot(
        activated,
        lax.all_gather(w_down, "expert", axis=1, tiled=True),
        preferred_element_type=jnp.float32,
    )
    returned = lax.all_to_all(partial_value, "mp", split_axis=1, concat_axis=0, tiled=True)
    expert_out = jnp.sum(returned.reshape(EXPERTS, copies, capacity, feat_local), axis=1).reshape(
        EXPERTS * capacity, feat_local
    )
    picked = expert_out[destination].reshape(tok_rows, top_k, feat_local)
    weights = 1.0 / (1.0 + jnp.exp(router_logits[:, ::-1] - router_logits))
    branch = jnp.sum(picked * weights[:, :, None], axis=1)
    combined = attended.astype(jnp.float32) + branch
    squares = lax.psum(jnp.sum(combined * combined, axis=1), "mp")
    normed = (
        combined * norm_gain[None, :] * lax.rsqrt(squares / model_width + epsilon)[:, None]
    ).astype(jnp.bfloat16)
    everyone = lax.all_gather(normed, "expert", axis=0, tiled=True)
    return everyone[request_order]


def solution(mesh):
    placed = (
        P("expert", "mp"),
        P("mp", None),
        P("expert", None),
        P("expert", None),
        P("mp", "expert"),
        P("mp", "expert"),
        P("mp", "expert"),
        P("mp"),
        P("expert"),
    )
    return jax.shard_map(
        shards, mesh=mesh, in_specs=placed, out_specs=P("expert", "mp"), check_vma=False
    )
```

profile of v0, /device:TPU:1, one launch (start us, length us, event | category | flops | bytes accessed | tf_op | source)
XLA Modules:
  0.0 565.7 jit_solution(14208333560372502879)
XLA Ops:
  6.5 0.7 all-gather.5.cloned.1.call-update
  7.3 0.7 all-gather.7.cloned.1.call-update
  9.3 0.8 copy.42
  10.5 0.7 broadcast_multiply_fusion
  11.2 2.3 reduce-window.6
  14.6 133.1 %all-gather.5.cloned.1.call-done = bf16[512,2048]{0,1:T(8,128)(2,1)} async-done(((bf16[512,32]{0,1:T(8,128)(2,1)}), bf16[512,2048]{0,1:T(8,128)(2,1)}) %all-gather.5.cloned.1.call-update) | async-done | bytes 2097168 | tf_op jit(solution)/shard_map/all_gather | solution.py:33
  147.7 2.0 convolution_convert_fusion
  149.9 6.4 %scatter_custom_fusion = bf16[2048,32]{1,0:T(8,128)(2,1)S(1)} fusion(s32[1024]{0:T(1024)S(1)} %bitcast.48, bf16[512,32]{1,0:T(8,128)(2,1)S(1)} %copy.44, s32[1024]{0:T(1024)S(1)} %broadcast_clamp_fusion.1, bf16[]{:T(256)} %constant.10.clone.1), kind=kCustom, calls=%fused_computation.16 | custom fusion | bytes 131074 | tf_op jit(solution)/shard_map/scatter | solution.py:42
  156.5 1.2 broadcast_in_dim.10
  157.7 8.8 %all-to-all-start = ((bf16[256,64,32]{0,2,1:T(8,128)(2,1)}), bf16[256,64,32]{0,2,1:T(8,128)(2,1)S(1)}, u32[]{:S(2)}, u32[]{:S(2)}) async-start(bf16[256,64,32]{0,2,1:T(8,128)(2,1)} %bitcast.6), calls=%async_computation | async-start | bytes 2097152 | tf_op jit(solution)/shard_map/all_to_all | solution.py:46
  166.5 26.9 %all-gather.7.cloned.1.call-done = bf16[704,2048]{1,0:T(8,128)(2,1)} async-done(((bf16[704,256]{1,0:T(8,128)(2,1)}), bf16[704,2048]{1,0:T(8,128)(2,1)}) %all-gather.7.cloned.1.call-update) | async-done | bytes 2883600 | tf_op jit(solution)/shard_map/all_gather | solution.py:50
  193.4 12.3 %all-to-all-done = bf16[256,64,32]{0,2,1:T(8,128)(2,1)S(1)} async-done(((bf16[256,64,32]{0,2,1:T(8,128)(2,1)}), bf16[256,64,32]{0,2,1:T(8,128)(2,1)S(1)}, u32[]{:S(2)}, u32[]{:S(2)}) %all-to-all-start) | async-done | bytes 1048608 | tf_op jit(solution)/shard_map/all_to_all | solution.py:46
  205.6 2.7 fusion.16
  208.4 26.4 %all-gather.11.cloned.1.call-done = bf16[704,2048]{1,0:T(8,128)(2,1)} async-done(((bf16[704,256]{1,0:T(8,128)(2,1)}), bf16[704,2048]{1,0:T(8,128)(2,1)}) %all-gather.11.cloned.1.call-update) | async-done | bytes 2883600 | tf_op jit(solution)/shard_map/all_gather | solution.py:62
  234.8 41.3 %all-gather.9.cloned.1.call-done = bf16[704,2048]{1,0:T(8,128)(2,1)} async-done(((bf16[704,256]{1,0:T(8,128)(2,1)}), bf16[704,2048]{1,0:T(8,128)(2,1)}) %all-gather.9.cloned.1.call-update) | async-done | bytes 2883600 | tf_op jit(solution)/shard_map/all_gather | solution.py:56
  276.1 7.2 %fusion.1 = f32[256,2048]{0,1:T(8,128)} fusion(bf16[704,2048]{1,0:T(8,128)(2,1)} %all-gather.11.cloned.1.call-done, bf16[704,2048]{1,0:T(8,128)(2,1)} %all-gather.9.cloned.1.call-done, bf16[256,2048]{0,1:T(8,128)(2,1)S(1)} %bitcast.46, f32[256,704]{0,1:T(8,128)S(1)} %fusion.16), kind=kOutput, calls=%fused_computation.8 | convolution fusion | flops 1477476352 | bytes 9633792 | tf_op jit(solution)/shard_map/dot_general | solution.py:60
  283.4 15.6 %all-to-all-start.1 = ((f32[256,64,32]{0,2,1:T(8,128)}), f32[256,64,32]{0,2,1:T(8,128)S(1)}, u32[]{:S(2)}, u32[]{:S(2)}) async-start(f32[256,64,32]{0,2,1:T(8,128)} %bitcast.43), calls=%async_computation.1 | async-start | bytes 4194304 | tf_op jit(solution)/shard_map/all_to_all | solution.py:65
  299.4 91.4 %all-to-all-done.1 = f32[256,64,32]{0,2,1:T(8,128)S(1)} async-done(((f32[256,64,32]{0,2,1:T(8,128)}), f32[256,64,32]{0,2,1:T(8,128)S(1)}, u32[]{:S(2)}, u32[]{:S(2)}) %all-to-all-start.1) | async-done | bytes 2097184 | tf_op jit(solution)/shard_map/all_to_all | solution.py:65
  391.3 2.8 gather_fusion
  394.1 2.8 multiply_reduce_fusion
  397.1 118.5 %psum.7 = f32[512]{0:T(512)S(1)} all-reduce(f32[512]{0:T(512)S(1)} %multiply_reduce_fusion.1), channel_id=1, replica_groups=mesh['expert'=8,'mp'=64] {'mp'}, use_global_device_ids=true, to_apply=%region_7.8 | all-reduce | flops 512 | bytes 4096 | tf_op jit(solution)/shard_map/psum | solution.py:73
  515.6 41.0 %all_gather.19 = bf16[4096,32]{0,1:T(8,128)(2,1)S(1)} all-gather(bf16[512,32]{0,1:T(8,128)(2,1)S(1)} %multiply_convert_fusion), channel_id=1, replica_groups=mesh['expert'=8,'mp'=64] {'expert'}, dimensions={0}, use_global_device_ids=true | all-gather | bytes 294912 | tf_op jit(solution)/shard_map/all_gather | solution.py:77
  557.1 1.3 gather_fusion.1
  558.4 0.7 copy.52
  (43 shorter events, 4.6 us)
Async XLA Ops:
  6.5 141.2 %copy-start = (bf16[32,2048]{1,0:T(8,128)(2,1)S(1)}, bf16[32,2048]{1,0:T(8,128)(2,1)}, u32[]{:S(2)}) copy-start(bf16[32,2048]{1,0:T(8,128)(2,1)} %param.10) | copy-start | bytes 393220
  6.5 141.2 %all-gather.5.cloned.1.call-start = ((), (), s32[]{:S(2)}) async-start(), calls=%async_computation.2 | async-start | bytes 2129920 | tf_op jit(solution)/shard_map/all_gather | solution.py:33
  7.3 186.1 %all-gather.7.cloned.1.call-start = ((), (), s32[]{:S(2)}) async-start(), calls=%async_computation.3 | async-start | bytes 3244032 | tf_op jit(solution)/shard_map/all_gather | solution.py:50
  8.0 226.8 %all-gather.11.cloned.1.call-start = ((), (), s32[]{:S(2)}) async-start(), calls=%async_computation.5 | async-start | bytes 3244032 | tf_op jit(solution)/shard_map/all_gather | solution.py:62
  8.7 267.4 %all-gather.9.cloned.1.call-start = ((), (), s32[]{:S(2)}) async-start(), calls=%async_computation.4 | async-start | bytes 3244032 | tf_op jit(solution)/shard_map/all_gather | solution.py:56
  157.7 48.0 %all-to-all-start = ((bf16[256,64,32]{0,2,1:T(8,128)(2,1)}), bf16[256,64,32]{0,2,1:T(8,128)(2,1)S(1)}, u32[]{:S(2)}, u32[]{:S(2)}) async-start(bf16[256,64,32]{0,2,1:T(8,128)(2,1)} %bitcast.6), calls=%async_computation | async-start | bytes 2097152 | tf_op jit(solution)/shard_map/all_to_all | solution.py:46
  283.4 15.7 %copy-start.1 = (f32[512,2]{0,1:T(2,128)S(1)}, f32[512,2]{0,1:T(2,128)}, u32[]{:S(2)}) copy-start(f32[512,2]{0,1:T(2,128)} %param.12) | copy-start | bytes 12292
  283.4 16.0 %copy-start.2 = (s32[512]{0:T(512)S(1)}, s32[512]{0:T(512)}, u32[]{:S(2)}) copy-start(s32[512]{0:T(512)} %param.17) | copy-start | bytes 6148
  283.4 107.4 %all-to-all-start.1 = ((f32[256,64,32]{0,2,1:T(8,128)}), f32[256,64,32]{0,2,1:T(8,128)S(1)}, u32[]{:S(2)}, u32[]{:S(2)}) async-start(f32[256,64,32]{0,2,1:T(8,128)} %bitcast.43), calls=%async_computation.1 | async-start | bytes 4194304 | tf_op jit(solution)/shard_map/all_to_all | solution.py:65
  391.3 124.3 %copy-start.3 = (f32[32]{0:T(128)S(1)}, f32[32]{0:T(128)}, u32[]{:S(2)}) copy-start(f32[32]{0:T(128)} %param.16) | copy-start | bytes 388
Sparse Core Ops, SparseCore 0:
  10.3 137.3 all-gather.4
  149.8 43.5 all-gather.6
  195.5 39.2 all-gather.10
  236.8 39.2 all-gather.8
where the time goes:
time: 566 us
  waiting for transfers between devices  334 us (59%)
  blocking collectives  159 us (28%)
  starting transfers between devices  24.5 us (4%)
  local copies, waits for them, and re-layouts  16 us (3%)
  between operations  13.4 us (2%)
  matrix products  12 us (2%)
  other arithmetic  6.35 us (1%)
    all_gather x1, waiting for transfers between devices, shards(): lax.all_gather(context, 'mp', axis=1, tiled=True)  133 us
    psum x1, blocking collectives, shards(): squares = lax.psum(jnp.sum(combined * combined, axis=1), 'mp')  118 us
    all_to_all x1, waiting for transfers between devices, shards(): lax.all_to_all(partial_value, 'mp', split_axis=1, concat_axis=0, tiled=True)  91.4 us
    all_gather x1, waiting for transfers between devices, shards(): lax.all_gather(w_up, 'expert', axis=1, tiled=True)  41.3 us
    all_gather x1, blocking collectives, shards(): everyone = lax.all_gather(normed, 'expert', axis=0, tiled=True)  41 us
    all_gather x1, waiting for transfers between devices, shards(): lax.all_gather(w_gate, 'expert', axis=1, tiled=True)  26.9 us
    all_gather x1, waiting for transfers between devices, shards(): lax.all_gather(w_down, 'expert', axis=1, tiled=True)  26.4 us
    all_to_all x1, starting transfers between devices, shards(): lax.all_to_all(partial_value, 'mp', split_axis=1, concat_axis=0, tiled=True)  15.6 us
  transfers between devices with their start and end apart: 6, of which 6 were waited for; matrix products, arithmetic and copies ran while one was open for 3% of the time, Pallas kernels for 0%

commit v1 on v0

--- a/solution.py
+++ b/solution.py
@@ -6,6 +6,13 @@
 EXPERTS = 8
 CAP = 256
 epsilon = 1e-06
+
+
+def gather_over(block, axis, dim):
+    devices = lax.axis_size(axis)
+    blocks = jnp.stack([block for _ in range(devices)])
+    blocks = lax.all_to_all(blocks, axis, split_axis=0, concat_axis=0)
+    return jnp.concatenate(blocks, axis=dim)
 
 
 def slot_targets(routes, capacity, experts):
@@ -58,9 +65,7 @@
     )
     activated = (jax.nn.silu(gate_next) * up_next).astype(jnp.bfloat16)
     partial_value = jnp.dot(
-        activated,
-        lax.all_gather(w_down, "expert", axis=1, tiled=True),
-        preferred_element_type=jnp.float32,
+        activated, gather_over(w_down, "expert", 1), preferred_element_type=jnp.float32
     )
     returned = lax.all_to_all(partial_value, "mp", split_axis=1, concat_axis=0, tiled=True)
     expert_out = jnp.sum(returned.reshape(EXPERTS, copies, capacity, feat_local), axis=1).reshape(

time: 566 us -> 525 us (0.928)
  waiting for transfers between devices: 334 us -> 269 us
  local copies, waits for them, and re-layouts: 16 us -> 28.3 us
  starting transfers between devices: 24.5 us -> 35.3 us
    all_gather x1 -> x0, waiting for transfers between devices: 26.4 us -> none  [shards(): lax.all_gather(w_down, 'expert', axis=1, tiled=True)]
    all_gather x1, waiting for transfers between devices: 41.3 us -> 20 us  [shards(): lax.all_gather(w_up, 'expert', axis=1, tiled=True)]
    all_gather x1, waiting for transfers between devices: 133 us -> 122 us  [shards(): lax.all_gather(context, 'mp', axis=1, tiled=True)]
    all_to_all x0 -> x1, starting transfers between devices: none -> 10.5 us  [gather_over(): blocks = lax.all_to_all(blocks, axis, split_axis=0, concat_axis=0)]
    all_gather x1, waiting for transfers between devices: 26.9 us -> 16.4 us  [shards(): lax.all_gather(w_gate, 'expert', axis=1, tiled=True)]
  transfers between devices with their start and end apart: 6 -> 6, of which waited for: 6 -> 5; matrix products, arithmetic and copies ran while one was open for 3% -> 6% of each run, Pallas kernels for 0% -> 0%
where the time goes in v1:
time: 525 us; the launch traced here: 524 us
  waiting for transfers between devices  269 us (51%)
  blocking collectives  159 us (30%)
  starting transfers between devices  35.3 us (7%)
  local copies, waits for them, and re-layouts  28.3 us (5%)
  between operations  13.3 us (3%)
  matrix products  12.9 us (2%)
  other arithmetic  5.67 us (1%)
    all_gather x1, waiting for transfers between devices, shards(): lax.all_gather(context, 'mp', axis=1, tiled=True)  122 us
    psum x1, blocking collectives, shards(): squares = lax.psum(jnp.sum(combined * combined, axis=1), 'mp')  118 us
    all_to_all x1, waiting for transfers between devices, shards(): lax.all_to_all(partial_value, 'mp', split_axis=1, concat_axis=0, tiled=True)  91.4 us
    all_gather x1, blocking collectives, shards(): everyone = lax.all_gather(normed, 'expert', axis=0, tiled=True)  41 us
    all_gather x1, waiting for transfers between devices, shards(): lax.all_gather(w_up, 'expert', axis=1, tiled=True)  20 us
    all_to_all x1, waiting for transfers between devices, shards(): lax.all_to_all(outgoing, 'mp', split_axis=1, concat_axis=1, tiled=True)  17.5 us
    all_gather x1, waiting for transfers between devices, shards(): lax.all_gather(w_gate, 'expert', axis=1, tiled=True)  16.4 us
    all_to_all x1, starting transfers between devices, shards(): lax.all_to_all(partial_value, 'mp', split_axis=1, concat_axis=0, tiled=True)  15.6 us
  transfers between devices with their start and end apart: 6, of which 5 were waited for; matrix products, arithmetic and copies ran while one was open for 6% of the time, Pallas kernels for 0%

profile of v1, /device:TPU:1, one launch (start us, length us, event | category | flops | bytes accessed | tf_op | source)
XLA Modules:
  0.0 524.1 jit_solution(7279656313269970555)
XLA Ops:
  8.0 2.7 stack.2
  10.8 10.5 %all-to-all-start.1 = ((bf16[8,704,256]{2,1,0:T(8,128)(2,1)}), bf16[8,704,256]{2,1,0:T(8,128)(2,1)S(1)}, u32[]{:S(2)}, u32[]{:S(2)}) async-start(bf16[8,704,256]{2,1,0:T(8,128)(2,1)} %stack.2), calls=%async_computation.1 | async-start | bytes 5767168 | tf_op jit(solution)/shard_map/all_to_all | solution.py:14
  22.5 2.3 reduce-window.6
  26.0 121.7 %all-gather.4.cloned.1.call-done = bf16[512,2048]{0,1:T(8,128)(2,1)} async-done(((bf16[512,32]{0,1:T(8,128)(2,1)}), bf16[512,2048]{0,1:T(8,128)(2,1)}) %all-gather.4.cloned.1.call-update) | async-done | bytes 2097168 | tf_op jit(solution)/shard_map/all_gather | solution.py:40
  147.7 2.0 convolution_convert_fusion
  149.8 0.8 copy.47
  150.5 9.5 %scatter_custom_fusion = bf16[2048,32]{1,0:T(8,128)(2,1)S(1)} fusion(s32[1024]{0:T(1024)S(1)} %bitcast.69, bf16[512,32]{1,0:T(8,128)(2,1)} %copy.47, s32[1024]{0:T(1024)S(1)} %broadcast_clamp_fusion.1, bf16[]{:T(256)} %constant.10.clone.1), kind=kCustom, calls=%fused_computation.10 | custom fusion | bytes 131584 | tf_op jit(solution)/shard_map/scatter | solution.py:49
  160.0 0.8 copy.49
  160.8 2.0 broadcast_in_dim.10
  162.8 9.0 %all-to-all-start = ((bf16[256,64,32]{0,2,1:T(8,128)(2,1)}), bf16[256,64,32]{0,2,1:T(8,128)(2,1)}, u32[]{:S(2)}, u32[]{:S(2)}) async-start(bf16[256,64,32]{0,2,1:T(8,128)(2,1)} %bitcast.64), calls=%async_computation | async-start | bytes 2097152 | tf_op jit(solution)/shard_map/all_to_all | solution.py:53
  171.9 2.0 copy.66
  173.9 3.1 copy.51
  177.0 16.4 %all-gather.6.cloned.1.call-done = bf16[704,2048]{1,0:T(8,128)(2,1)} async-done(((bf16[704,256]{1,0:T(8,128)(2,1)}), bf16[704,2048]{1,0:T(8,128)(2,1)}) %all-gather.6.cloned.1.call-update) | async-done | bytes 2883600 | tf_op jit(solution)/shard_map/all_gather | solution.py:57
  193.4 17.5 %all-to-all-done = bf16[256,64,32]{0,2,1:T(8,128)(2,1)} async-done(((bf16[256,64,32]{0,2,1:T(8,128)(2,1)}), bf16[256,64,32]{0,2,1:T(8,128)(2,1)}, u32[]{:S(2)}, u32[]{:S(2)}) %all-to-all-start) | async-done | bytes 1048608 | tf_op jit(solution)/shard_map/all_to_all | solution.py:53
  210.9 3.9 fusion.10
  214.8 20.0 %all-gather.8.cloned.1.call-done = bf16[704,2048]{1,0:T(8,128)(2,1)} async-done(((bf16[704,256]{1,0:T(8,128)(2,1)}), bf16[704,2048]{1,0:T(8,128)(2,1)}) %all-gather.8.cloned.1.call-update) | async-done | bytes 2883600 | tf_op jit(solution)/shard_map/all_gather | solution.py:63
  234.8 6.9 %fusion.9 = f32[256,64,32]{0,2,1:T(8,128)} fusion(bf16[64,32,704]{2,1,0:T(8,128)(2,1)S(1)} %bitcast.65, bf16[704,2048]{1,0:T(8,128)(2,1)} %all-gather.8.cloned.1.call-done, bf16[256,2048]{0,1:T(8,128)(2,1)} %bitcast.7, f32[256,704]{0,1:T(8,128)} %fusion.10), kind=kOutput, calls=%fused_computation.34 | convolution fusion | flops 1477476352 | bytes 9633792 | tf_op jit(solution)/shard_map/dot_general | solution.py:67
  241.7 15.6 %all-to-all-start.2 = ((f32[256,64,32]{0,2,1:T(8,128)}), f32[256,64,32]{0,2,1:T(8,128)S(1)}, u32[]{:S(2)}, u32[]{:S(2)}) async-start(f32[256,64,32]{0,2,1:T(8,128)} %fusion.9), calls=%async_computation.2 | async-start | bytes 4194304 | tf_op jit(solution)/shard_map/all_to_all | solution.py:70
  257.7 91.4 %all-to-all-done.2 = f32[256,64,32]{0,2,1:T(8,128)S(1)} async-done(((f32[256,64,32]{0,2,1:T(8,128)}), f32[256,64,32]{0,2,1:T(8,128)S(1)}, u32[]{:S(2)}, u32[]{:S(2)}) %all-to-all-start.2) | async-done | bytes 2097184 | tf_op jit(solution)/shard_map/all_to_all | solution.py:70
  349.7 2.8 gather_fusion
  352.5 2.8 multiply_reduce_fusion
  355.4 118.5 %psum.7 = f32[512]{0:T(512)S(1)} all-reduce(f32[512]{0:T(512)S(1)} %multiply_reduce_fusion.1), channel_id=1, replica_groups=mesh['expert'=8,'mp'=64] {'mp'}, use_global_device_ids=true, to_apply=%region_7.8 | all-reduce | flops 512 | bytes 4096 | tf_op jit(solution)/shard_map/psum | solution.py:78
  474.0 41.0 %all_gather.15 = bf16[4096,32]{0,1:T(8,128)(2,1)S(1)} all-gather(bf16[512,32]{0,1:T(8,128)(2,1)S(1)} %multiply_convert_fusion), channel_id=1, replica_groups=mesh['expert'=8,'mp'=64] {'expert'}, dimensions={0}, use_global_device_ids=true | all-gather | bytes 294912 | tf_op jit(solution)/shard_map/all_gather | solution.py:82
  515.5 1.3 gather_fusion.1
  (51 shorter events, 6.0 us)
Async XLA Ops:
  6.5 141.2 %copy-start = (bf16[32,2048]{1,0:T(8,128)(2,1)S(1)}, bf16[32,2048]{1,0:T(8,128)(2,1)}, u32[]{:S(2)}) copy-start(bf16[32,2048]{1,0:T(8,128)(2,1)} %param.10) | copy-start | bytes 393220
  6.5 141.2 %all-gather.4.cloned.1.call-start = ((), (), s32[]{:S(2)}) async-start(), calls=%async_computation.3 | async-start | bytes 2129920 | tf_op jit(solution)/shard_map/all_gather | solution.py:40
  7.3 186.1 %all-gather.6.cloned.1.call-start = ((), (), s32[]{:S(2)}) async-start(), calls=%async_computation.4 | async-start | bytes 3244032 | tf_op jit(solution)/shard_map/all_gather | solution.py:57
  10.8 11.3 %copy-start.3 = (s32[512,2]{0,1:T(2,128)S(1)}, s32[512,2]{0,1:T(2,128)}, u32[]{:S(2)}) copy-start(s32[512,2]{0,1:T(2,128)} %param.11) | copy-start | bytes 12292
  10.8 150.1 %all-to-all-start.1 = ((bf16[8,704,256]{2,1,0:T(8,128)(2,1)}), bf16[8,704,256]{2,1,0:T(8,128)(2,1)S(1)}, u32[]{:S(2)}, u32[]{:S(2)}) async-start(bf16[8,704,256]{2,1,0:T(8,128)(2,1)} %stack.2), calls=%async_computation.1 | async-start | bytes 5767168 | tf_op jit(solution)/shard_map/all_to_all | solution.py:14
  21.3 213.5 %all-gather.8.cloned.1.call-start = ((), (), s32[]{:S(2)}) async-start(), calls=%async_computation.5 | async-start | bytes 3244032 | tf_op jit(solution)/shard_map/all_gather | solution.py:63
  149.7 0.8 copy-start.1
  162.8 48.0 %all-to-all-start = ((bf16[256,64,32]{0,2,1:T(8,128)(2,1)}), bf16[256,64,32]{0,2,1:T(8,128)(2,1)}, u32[]{:S(2)}, u32[]{:S(2)}) async-start(bf16[256,64,32]{0,2,1:T(8,128)(2,1)} %bitcast.64), calls=%async_computation | async-start | bytes 2097152 | tf_op jit(solution)/shard_map/all_to_all | solution.py:53
  241.7 15.7 %copy-start.4 = (f32[512,2]{0,1:T(2,128)S(1)}, f32[512,2]{0,1:T(2,128)}, u32[]{:S(2)}) copy-start(f32[512,2]{0,1:T(2,128)} %param.12) | copy-start | bytes 12292
  241.7 16.0 %copy-start.5 = (s32[512]{0:T(512)S(1)}, s32[512]{0:T(512)}, u32[]{:S(2)}) copy-start(s32[512]{0:T(512)} %param.17) | copy-start | bytes 6148
  241.7 107.4 %all-to-all-start.2 = ((f32[256,64,32]{0,2,1:T(8,128)}), f32[256,64,32]{0,2,1:T(8,128)S(1)}, u32[]{:S(2)}, u32[]{:S(2)}) async-start(f32[256,64,32]{0,2,1:T(8,128)} %fusion.9), calls=%async_computation.2 | async-start | bytes 4194304 | tf_op jit(solution)/shard_map/all_to_all | solution.py:70
  349.6 5.8 %copy-start.2 = (bf16[512,32]{0,1:T(8,128)(2,1)S(1)}, bf16[512,32]{0,1:T(8,128)(2,1)}, u32[]{:S(2)}) copy-start(bf16[512,32]{0,1:T(8,128)(2,1)} %copy-done.1) | copy-start | bytes 98308
  349.7 124.3 %copy-start.6 = (f32[32]{0:T(128)S(1)}, f32[32]{0:T(128)}, u32[]{:S(2)}) copy-start(f32[32]{0:T(128)} %param.16) | copy-start | bytes 388
Sparse Core Ops, SparseCore 0:
  10.3 137.3 all-gather.3
  149.8 43.5 all-gather.5
  195.5 39.2 all-gather.7
